TPU v7x, 128 devices: a whole 4x4x4 slice. The times are simulated.
128 devices in a mesh: row: 16 (over z_lo, x, core), col: 8 (over y, z_hi).
Axes of the slice: x: 4, y: 4, z: 4 (z_hi: 2, z_lo: 2; z = z_hi * 2 + z_lo), core: 2. Of those that a mesh axis runs over, the one named last changes fastest.
Arguments:
- slab_embed: float32 [65536, 768], P(('col', 'row')), may hold values from -1 to 1
- coverage_old: float32 [65536], P('col'), may hold values from 2 to 4.5
- sel_index: int32 [2048], P('row'), may hold values from 0 to 65535
- cand_index: int32 [3072], P('row'), may hold values from 0 to 65535
Outputs:
- coverage: float32 [65536], P('col')
- total_gain: float32 [3072], P('row')
Inputs may be any that keep to these rules, and one draw needn't show every extreme that they name: `sel_index`: indices into the slab. `cand_index`: indices into the slab.
All inputs are finite; a program needn't handle non-finite values.
Results may differ from a plain program's by a relative error of at most 0.00014.
Values sent between devices are 32-bit elements; how exact they have to be, the bound alone decides.
No kernel may reach another device: no remote copies, remote signals or barrier semaphores. Data moves between devices by JAX's collectives and lax.ppermute only.
A program may use at most 128 MiB of HBM per device.

v0:
```python
import jax
import jax.numpy as jnp
from jax import lax
from jax.sharding import PartitionSpec as P


def similar(left, right):
    return lax.dot_general(
        left,
        right,
        (((1,), (1,)), ((), ())),
        precision=lax.Precision.HIGH,
        preferred_element_type=jnp.float32,
    )


def lookup(source, indices, first_row):
    position = indices - first_row
    inside = (position >= 0) & (position < source.shape[0])
    picked = jnp.take(source, jnp.clip(position, 0, source.shape[0] - 1), axis=0)
    return jnp.where(inside[:, None], picked, 0.0)


def shift(value, axis, size, pairs):
    return lax.ppermute(value, axis, [(i, j) for i, j in pairs if i < size and j < size])


def col_parts(value, n_y, n_z):
    size = n_y * n_z
    here = lax.axis_index("col")
    y, z = (here // n_z, here % n_z)
    if n_z == 2:
        other = shift(value, "col", size, [(c, c ^ 1) for c in range(size)])
        pair = jnp.where(z == 0, jnp.stack([value, other]), jnp.stack([other, value]))
    else:
        pair = value[None]
    if n_y == 1:
        return pair
    up = [(c, (c // n_z + 1) % n_y * n_z + c % n_z) for c in range(size)]
    down = [(c, (c // n_z - 1) % n_y * n_z + c % n_z) for c in range(size)]
    from_below = shift(pair, "col", size, up)
    from_above = shift(pair, "col", size, down)
    parts = [pair, from_above, None, from_below]
    if n_y == 4:
        parts[2] = shift(from_below, "col", size, up)
        ordered = jnp.stack(parts)
    else:
        ordered = jnp.stack([pair, from_above])
    return jnp.roll(ordered, y, axis=0).reshape((size,) + value.shape)


def col_masked_sum(value, n_y, n_z):
    size = n_y * n_z
    if n_z == 2:
        value = value + shift(value, "col", size, [(c, c ^ 1) for c in range(size)])
    up = [(c, (c // n_z + 1) % n_y * n_z + c % n_z) for c in range(size)]
    down = [(c, (c // n_z - 1) % n_y * n_z + c % n_z) for c in range(size)]
    from_below = shift(value, "col", size, up)
    from_above = shift(value, "col", size, down)
    far = shift(from_below, "col", size, up)
    return value + from_below + from_above + far


def row_max(value, n):
    here = lax.axis_index("row")
    value = jnp.maximum(value, shift(value, "row", n, [(r, r ^ 1) for r in range(n)]))
    x_up = [(r, r & ~6 | ((r >> 1 & 3) + 1) % 4 << 1) for r in range(n)]
    x_down = [(r, r & ~6 | ((r >> 1 & 3) - 1) % 4 << 1) for r in range(n)]
    value = jnp.maximum(
        value, jnp.maximum(shift(value, "row", n, x_up), shift(value, "row", n, x_down))
    )
    value = jnp.maximum(value, shift(value, "row", n, x_up))
    value = jnp.maximum(value, shift(value, "row", n, [(r, r ^ 8) for r in range(n)]))
    return value


def body(slab_embed, coverage_old, sel_index, cand_index):
    col_id = lax.axis_index("col")
    gathered = lax.all_gather(slab_embed, "row", axis=0, tiled=True)
    first_row = col_id * gathered.shape[0]
    n_sel = sel_index.shape[0]
    picked = col_masked_sum(
        jnp.concatenate(
            [lookup(gathered, sel_index, first_row), lookup(gathered, cand_index, first_row)]
        ),
        4,
        2,
    )
    selected, chosen = (picked[:n_sel], picked[n_sel:])
    partial_value = jnp.max(similar(selected, gathered), axis=0)
    reached = row_max(partial_value, 16)
    coverage = jnp.maximum(coverage_old, reached)
    gain_part = jnp.sum(jnp.maximum(similar(chosen, gathered) - coverage[None, :], 0.0), axis=1)
    total_gain = jnp.sum(col_parts(gain_part, 4, 2), axis=0)
    return (coverage, total_gain)


def solution(mesh):
    in_specs = (P(("col", "row"), None), P("col"), P("row"), P("row"))
    out_specs = (P("col"), P("row"))
    return jax.shard_map(body, mesh=mesh, in_specs=in_specs, out_specs=out_specs, check_vma=False)
```

profile of v0, /device:TPU:0, one launch (start us, length us, event | category | flops | bytes accessed | tf_op | source)
XLA Modules:
  0.0 307.7 jit_solution(16716492885634201981)
XLA Ops:
  7.2 0.7 all-gather.2.cloned.1.call-update
  7.9 0.7 compare_and_fusion
  8.6 0.7 compare_and_fusion.2
  9.3 134.1 %all-gather.2.cloned.1.call-done = f32[8192,768]{1,0:T(8,128)} async-done(((f32[512,768]{1,0:T(8,128)}), f32[8192,768]{1,0:T(8,128)}) %all-gather.2.cloned.1.call-update) | async-done | bytes 25165840 | tf_op jit(solution)/shard_map/all_gather | solution.py:79
  143.4 9.3 %gather_fusion.1 = f32[192,768]{1,0:T(8,128)S(1)} fusion(f32[8192,768]{1,0:T(8,128)} %all-gather.2.cloned.1.call-done, s32[1024]{0:T(1024)S(1)} %pad_clamp_fusion), kind=kCustom, calls=%fused_computation.1 | custom fusion | bytes 1180416 | tf_op jit(solution)/shard_map/jit(_take)/gather | solution.py:20
  152.7 0.1 select_select_fusion
  152.9 9.1 %gather_fusion = f32[128,768]{1,0:T(8,128)S(1)} fusion(f32[8192,768]{1,0:T(8,128)} %all-gather.2.cloned.1.call-done, s32[1024]{0:T(1024)S(1)} %pad_clamp_fusion.1), kind=kCustom, calls=%fused_computation | custom fusion | bytes 786944 | tf_op jit(solution)/shard_map/jit(_take)/gather | solution.py:20
  162.0 0.1 select_select_fusion.1
  162.2 2.9 collective-permute-start
  165.1 22.6 %collective-permute-done = f32[320,768]{1,0:T(8,128)S(1)} collective-permute-done((f32[320,768]{1,0:T(8,128)S(1)}, f32[320,768]{1,0:T(8,128)S(1)}, u32[]{:S(2)}, u32[]{:S(2)}) %collective-permute-start) | collective-permute-done | bytes 983072 | tf_op jit(solution)/shard_map/ppermute | solution.py:25
  187.8 1.6 collective-permute-start.1
  189.4 1.8 collective-permute-start.2
  191.1 21.1 %collective-permute-done.1 = f32[320,768]{1,0:T(8,128)S(1)} collective-permute-done((f32[320,768]{1,0:T(8,128)S(1)}, f32[320,768]{1,0:T(8,128)S(1)}, u32[]{:S(2)}, u32[]{:S(2)}) %collective-permute-start.1) | collective-permute-done | bytes 983072 | tf_op jit(solution)/shard_map/ppermute | solution.py:25
  212.2 0.3 collective-permute-start.3
  212.5 23.1 %collective-permute-done.3 = f32[320,768]{1,0:T(8,128)S(1)} collective-permute-done((f32[320,768]{1,0:T(8,128)S(1)}, f32[320,768]{1,0:T(8,128)S(1)}, u32[]{:S(2)}, u32[]{:S(2)}) %collective-permute-start.3) | collective-permute-done | bytes 983072 | tf_op jit(solution)/shard_map/ppermute | solution.py:25
  235.6 0.3 add_add_fusion
  235.9 16.5 %convolution_reduce_fusion = f32[8192]{0:T(1024)S(1)} fusion(f32[8192,768]{1,0:T(8,128)} %all-gather.2.cloned.1.call-done, f32[320,768]{1,0:T(8,128)S(1)} %add_add_fusion), kind=kOutput, calls=%fused_computation.5 | convolution fusion | flops 4832878592 | bytes 25591808 | tf_op jit(solution)/shard_map/dot_general | solution.py:8
  252.5 1.2 collective-permute-done.4
  253.7 1.1 collective-permute-start.5
  254.8 2.1 collective-permute-start.6
  256.9 1.9 collective-permute-done.5
  258.8 1.1 collective-permute-start.7
  260.0 4.1 %collective-permute-done.7 = f32[8192]{0:T(1024)S(1)} collective-permute-done((f32[8192]{0:T(1024)S(1)}, f32[8192]{0:T(1024)S(1)}, u32[]{:S(2)}, u32[]{:S(2)}) %collective-permute-start.7) | collective-permute-done | bytes 32800 | tf_op jit(solution)/shard_map/ppermute | solution.py:25
  264.0 1.7 collective-permute-start.8
  265.8 2.2 collective-permute-done.8
  268.0 17.4 %fusion.1 = f32[192]{0:T(256)S(1)} fusion(f32[8192]{0:T(1024)S(1)} %maximum_maximum_fusion, f32[8192,768]{1,0:T(8,128)} %all-gather.2.cloned.1.call-done, f32[320,768]{1,0:T(8,128)S(1)} %add_add_fusion), kind=kOutput, calls=%fused_computation.4 | convolution fusion | flops 7252475904 | bytes 25789184 | tf_op jit(solution)/shard_map/dot_general | solution.py:8
  285.4 3.1 %collective-permute-start.9 = (f32[192]{0:T(256)S(1)}, f32[192]{0:T(256)S(1)}, u32[]{:S(2)}, u32[]{:S(2)}) collective-permute-start(f32[192]{0:T(256)S(1)} %fusion.1), channel_id=1, source_target_pairs={{0,1},{1,0},{2,3},{3,2},{4,5},{5,4},{6,7},{7,6},{8,9},{9,8},{10,11... | collective-permute-start | bytes 2312 | tf_op jit(solution)/shard_map/ppermute | solution.py:25
  288.5 2.0 collective-permute-done.9
  290.7 3.2 %collective-permute-start.10 = (f32[2,192]{1,0:T(2,128)S(1)}, f32[2,192]{1,0:T(2,128)S(1)}, u32[]{:S(2)}, u32[]{:S(2)}) collective-permute-start(f32[2,192]{1,0:T(2,128)S(1)} %maximum_select_fusion), channel_id=1, source_target_pairs={{0,6},{1,7},{2,0},{3,1},{4,2},{5,3},{6,4},{7,5},{8,14},{9,15},{10,... | collective-permute-start | bytes 4616 | tf_op jit(solution)/shard_map/ppermute | solution.py:25
  293.8 1.6 collective-permute-done.11
  295.5 4.8 %collective-permute-done.12 = f32[2,192]{1,0:T(2,128)S(1)} collective-permute-done((f32[2,192]{1,0:T(2,128)S(1)}, f32[2,192]{1,0:T(2,128)S(1)}, u32[]{:S(2)}, u32[]{:S(2)}) %collective-permute-start.12) | collective-permute-done | bytes 1568 | tf_op jit(solution)/shard_map/ppermute | solution.py:25
  300.2 0.6 dynamic-slice_reduce_fusion
  (25 shorter events, 0.5 us)
Async XLA Ops:
  7.2 136.2 %all-gather.2.cloned.1.call-start = ((), (), s32[]{:S(2)}) async-start(), calls=%async_computation | async-start | bytes 26738688 | tf_op jit(solution)/shard_map/all_gather | solution.py:79
  152.7 115.2 %copy-start.1 = (f32[8192]{0:T(1024)S(1)}, f32[8192]{0:T(1024)}, u32[]{:S(2)}) copy-start(f32[8192]{0:T(1024)} %param.5) | copy-start | bytes 98308
  162.2 25.5 %collective-permute-start = (f32[320,768]{1,0:T(8,128)S(1)}, f32[320,768]{1,0:T(8,128)S(1)}, u32[]{:S(2)}, u32[]{:S(2)}) collective-permute-start(f32[320,768]{1,0:T(8,128)S(1)} %pad_maximum_fusion), channel_id=1, source_target_pairs={{0,1},{1,0},{2,3},{3,2},{4,5},{5,4},{6,7},{7,6},{8,9},{9,8},{10,11... | collective-permute-start | bytes 2949128 | tf_op jit(solution)/shard_map/ppermute | solution.py:25
  187.8 24.4 %collective-permute-start.1 = (f32[320,768]{1,0:T(8,128)S(1)}, f32[320,768]{1,0:T(8,128)S(1)}, u32[]{:S(2)}, u32[]{:S(2)}) collective-permute-start(f32[320,768]{1,0:T(8,128)S(1)} %fusion.4), channel_id=1, source_target_pairs={{0,2},{1,3},{2,4},{3,5},{4,6},{5,7},{6,0},{7,1},{8,10},{9,11},{10,... | collective-permute-start | bytes 2949128 | tf_op jit(solution)/shard_map/ppermute | solution.py:25
  189.4 23.1 %collective-permute-start.2 = (f32[320,768]{1,0:T(8,128)S(1)}, f32[320,768]{1,0:T(8,128)S(1)}, u32[]{:S(2)}, u32[]{:S(2)}) collective-permute-start(f32[320,768]{1,0:T(8,128)S(1)} %fusion.4), channel_id=1, source_target_pairs={{0,6},{1,7},{2,0},{3,1},{4,2},{5,3},{6,4},{7,5},{8,14},{9,15},{10,... | collective-permute-start | bytes 2949128 | tf_op jit(solution)/shard_map/ppermute | solution.py:25
  212.2 23.4 %collective-permute-start.3 = (f32[320,768]{1,0:T(8,128)S(1)}, f32[320,768]{1,0:T(8,128)S(1)}, u32[]{:S(2)}, u32[]{:S(2)}) collective-permute-start(f32[320,768]{1,0:T(8,128)S(1)} %collective-permute-done.1), channel_id=1, source_target_pairs={{0,2},{1,3},{2,4},{3,5},{4,6},{5,7},{6,0},{7,1},{8,10},{9,11},{10,... | collective-permute-start | bytes 2949128 | tf_op jit(solution)/shard_map/ppermute | solution.py:25
  252.4 1.3 collective-permute-start.4
  253.7 5.1 %collective-permute-start.5 = (f32[8192]{0:T(1024)S(1)}, f32[8192]{0:T(1024)S(1)}, u32[]{:S(2)}, u32[]{:S(2)}) collective-permute-start(f32[8192]{0:T(1024)S(1)} %max.32), channel_id=1, source_target_pairs={{0,16},{8,24},{16,32},{24,40},{32,48},{40,56},{48,0},{56,8},{64,80... | collective-permute-start | bytes 98312 | tf_op jit(solution)/shard_map/ppermute | solution.py:25
  254.8 4.0 %collective-permute-start.6 = (f32[8192]{0:T(1024)S(1)}, f32[8192]{0:T(1024)S(1)}, u32[]{:S(2)}, u32[]{:S(2)}) collective-permute-start(f32[8192]{0:T(1024)S(1)} %max.32), channel_id=1, source_target_pairs={{0,48},{8,56},{16,0},{24,8},{32,16},{40,24},{48,32},{56,40},{64,11... | collective-permute-start | bytes 98312 | tf_op jit(solution)/shard_map/ppermute | solution.py:25
  258.8 5.2 %collective-permute-start.7 = (f32[8192]{0:T(1024)S(1)}, f32[8192]{0:T(1024)S(1)}, u32[]{:S(2)}, u32[]{:S(2)}) collective-permute-start(f32[8192]{0:T(1024)S(1)} %maximum_maximum_fusion.1), channel_id=1, source_target_pairs={{0,16},{8,24},{16,32},{24,40},{32,48},{40,56},{48,0},{56,8},{64,80... | collective-permute-start | bytes 98312 | tf_op jit(solution)/shard_map/ppermute | solution.py:25
  264.0 3.9 %collective-permute-start.8 = (f32[8192]{0:T(1024)S(1)}, f32[8192]{0:T(1024)S(1)}, u32[]{:S(2)}, u32[]{:S(2)}) collective-permute-start(f32[8192]{0:T(1024)S(1)} %max.35), channel_id=1, source_target_pairs={{0,64},{8,72},{16,80},{24,88},{32,96},{40,104},{48,112},{56,120},{... | collective-permute-start | bytes 98312 | tf_op jit(solution)/shard_map/ppermute | solution.py:25
  268.0 32.9 %copy-start = (f32[8192]{0:T(1024)}, f32[8192]{0:T(1024)S(1)}, u32[]{:S(2)}) copy-start(f32[8192]{0:T(1024)S(1)} %maximum_maximum_fusion) | copy-start | bytes 98308
  285.4 5.2 %collective-permute-start.9 = (f32[192]{0:T(256)S(1)}, f32[192]{0:T(256)S(1)}, u32[]{:S(2)}, u32[]{:S(2)}) collective-permute-start(f32[192]{0:T(256)S(1)} %fusion.1), channel_id=1, source_target_pairs={{0,1},{1,0},{2,3},{3,2},{4,5},{5,4},{6,7},{7,6},{8,9},{9,8},{10,11... | collective-permute-start | bytes 2312 | tf_op jit(solution)/shard_map/ppermute | solution.py:25
  290.5 4.9 %collective-permute-start.11 = (f32[2,192]{1,0:T(2,128)S(1)}, f32[2,192]{1,0:T(2,128)S(1)}, u32[]{:S(2)}, u32[]{:S(2)}) collective-permute-start(f32[2,192]{1,0:T(2,128)S(1)} %maximum_select_fusion), channel_id=1, source_target_pairs={{0,2},{1,3},{2,4},{3,5},{4,6},{5,7},{6,0},{7,1},{8,10},{9,11},{10,... | collective-permute-start | bytes 4616 | tf_op jit(solution)/shard_map/ppermute | solution.py:25
  290.7 4.8 %collective-permute-start.10 = (f32[2,192]{1,0:T(2,128)S(1)}, f32[2,192]{1,0:T(2,128)S(1)}, u32[]{:S(2)}, u32[]{:S(2)}) collective-permute-start(f32[2,192]{1,0:T(2,128)S(1)} %maximum_select_fusion), channel_id=1, source_target_pairs={{0,6},{1,7},{2,0},{3,1},{4,2},{5,3},{6,4},{7,5},{8,14},{9,15},{10,... | collective-permute-start | bytes 4616 | tf_op jit(solution)/shard_map/ppermute | solution.py:25
  295.4 4.8 %collective-permute-start.12 = (f32[2,192]{1,0:T(2,128)S(1)}, f32[2,192]{1,0:T(2,128)S(1)}, u32[]{:S(2)}, u32[]{:S(2)}) collective-permute-start(f32[2,192]{1,0:T(2,128)S(1)} %collective-permute-done.11), channel_id=1, source_target_pairs={{0,2},{1,3},{2,4},{3,5},{4,6},{5,7},{6,0},{7,1},{8,10},{9,11},{10,... | collective-permute-start | bytes 4616 | tf_op jit(solution)/shard_map/ppermute | solution.py:25
Sparse Core Ops, SparseCore 0:
  9.7 133.6 all-gather.1
where the time goes:
time: 308 us
  waiting for transfers between devices  219 us (71%)
  matrix products  33.9 us (11%)
  starting transfers between devices  19.1 us (6%)
  local copies, waits for them, and re-layouts  18.5 us (6%)
  between operations  14.2 us (5%)
    all_gather x1, waiting for transfers between devices, body(): gathered = lax.all_gather(slab_embed, 'row', axis=0, tiled=True)  134 us
    ppermute x13, waiting for transfers between devices, shift(): lax.ppermute(value, axis, [(i, j) for i, j in pairs if i < size and j < s...  84.5 us
    dot_general x2, matrix products, similar(): lax.dot_general(left, right, (((1,), (1,)), ((), ())), precision=lax.Prec...  33.9 us
    ppermute x13, starting transfers between devices, shift(): lax.ppermute(value, axis, [(i, j) for i, j in pairs if i < size and j < s...  19.1 us
    gather x2, local copies, waits for them, and re-layouts, lookup(): jnp.take(source, jnp.clip(position, 0, source.shape[0] - 1), axis=0)  18.5 us
  transfers between devices with their start and end apart: 14, of which 11 were waited for; matrix products, arithmetic and copies ran while one was open for 0% of the time, Pallas kernels for 0%

commit v1 on v0

--- a/solution.py
+++ b/solution.py
@@ -2,6 +2,16 @@
 import jax.numpy as jnp
 from jax import lax
 from jax.sharding import PartitionSpec as P
+
+
+def post_the_sector(t0, comm_axis):
+    front = jnp.concatenate(
+        jax.lax.all_to_all(
+            jnp.stack([t0] * jax.lax.axis_size(comm_axis)), comm_axis, split_axis=0, concat_axis=0
+        ),
+        0,
+    )
+    return front
 
 
 def similar(left, right):
@@ -76,7 +86,7 @@
 
 def body(slab_embed, coverage_old, sel_index, cand_index):
     col_id = lax.axis_index("col")
-    gathered = lax.all_gather(slab_embed, "row", axis=0, tiled=True)
+    gathered = post_the_sector(slab_embed, "row")
     first_row = col_id * gathered.shape[0]
     n_sel = sel_index.shape[0]
     picked = col_masked_sum(

time: 308 us -> 514 us (1.67)
  waiting for transfers between devices: 219 us -> 425 us
  between operations: 14.2 us -> 0.86 us
  local copies, waits for them, and re-layouts: 18.5 us -> 30.7 us
    all_to_all x0 -> x1, waiting for transfers between devices: none -> 337 us  [post_the_sector(): jax.lax.all_to_all(jnp.stack([t0] * jax.lax.axis_size(comm_axis)), comm_a...]
    all_gather x1 -> x0, waiting for transfers between devices: 134 us -> none  [body(): gathered = lax.all_gather(slab_embed, 'row', axis=0, tiled=True)]
    another operation x0 -> x1, local copies, waits for them, and re-layouts: none -> 12.1 us  [post_the_sector(): jnp.stack([t0] * jax.lax.axis_size(comm_axis))]
    all_to_all x0 -> x1, starting transfers between devices: none -> 6.02 us  [post_the_sector(): jax.lax.all_to_all(jnp.stack([t0] * jax.lax.axis_size(comm_axis)), comm_a...]
  transfers between devices with their start and end apart: 14 -> 14, of which waited for: 11 -> 12; matrix products, arithmetic and copies ran while one was open for 0% -> 0% of each run, Pallas kernels for 0% -> 0%
where the time goes in v1:
time: 514 us
  waiting for transfers between devices  425 us (83%)
  matrix products  33.9 us (7%)
  local copies, waits for them, and re-layouts  30.7 us (6%)
  starting transfers between devices  22.7 us (4%)
    all_to_all x1, waiting for transfers between devices, post_the_sector(): jax.lax.all_to_all(jnp.stack([t0] * jax.lax.axis_size(comm_axis)), comm_a...  337 us
    ppermute x13, waiting for transfers between devices, shift(): lax.ppermute(value, axis, [(i, j) for i, j in pairs if i < size and j < s...  88 us
    dot_general x2, matrix products, similar(): lax.dot_general(left, right, (((1,), (1,)), ((), ())), precision=lax.Prec...  33.9 us
    gather x2, local copies, waits for them, and re-layouts, lookup(): jnp.take(source, jnp.clip(position, 0, source.shape[0] - 1), axis=0)  18.5 us
    ppermute x13, starting transfers between devices, shift(): lax.ppermute(value, axis, [(i, j) for i, j in pairs if i < size and j < s...  16.7 us
    another operation x1, local copies, waits for them, and re-layouts, post_the_sector(): jnp.stack([t0] * jax.lax.axis_size(comm_axis))  12.1 us
  transfers between devices with their start and end apart: 14, of which 12 were waited for; matrix products, arithmetic and copies ran while one was open for 0% of the time, Pallas kernels for 0%

profile of v1, /device:TPU:0, one launch (start us, length us, event | category | flops | bytes accessed | tf_op | source)
XLA Modules:
  0.0 514.2 jit_solution(3262516847430330431)
XLA Ops:
  0.6 12.1 %stack.24 = f32[16,512,768]{2,1,0:T(8,128)} broadcast(f32[512,768]{1,0:T(8,128)} %param.4), dimensions={1,2} | broadcast | bytes 26738688 | tf_op jit(solution)/shard_map/stack | solution.py:10
  12.8 6.0 %all-to-all-start = ((f32[16,512,768]{2,1,0:T(8,128)}), f32[16,512,768]{2,1,0:T(8,128)}, u32[]{:S(2)}, u32[]{:S(2)}) async-start(f32[16,512,768]{2,1,0:T(8,128)} %stack.24), calls=%async_computation | async-start | bytes 50331648 | tf_op jit(solution)/shard_map/all_to_all | solution.py:9
  18.9 336.7 %all-to-all-done = f32[16,512,768]{2,1,0:T(8,128)} async-done(((f32[16,512,768]{2,1,0:T(8,128)}), f32[16,512,768]{2,1,0:T(8,128)}, u32[]{:S(2)}, u32[]{:S(2)}) %all-to-all-start) | async-done | bytes 25165856 | tf_op jit(solution)/shard_map/all_to_all | solution.py:9
  355.6 9.3 %gather_fusion.1 = f32[192,768]{1,0:T(8,128)S(1)} fusion(f32[8192,768]{1,0:T(8,128)} %bitcast, s32[1024]{0:T(1024)S(1)} %pad_clamp_fusion), kind=kCustom, calls=%fused_computation.1 | custom fusion | bytes 1180416 | tf_op jit(solution)/shard_map/jit(_take)/gather | solution.py:30
  365.0 9.1 %gather_fusion = f32[128,768]{1,0:T(8,128)S(1)} fusion(f32[8192,768]{1,0:T(8,128)} %bitcast, s32[1024]{0:T(1024)S(1)} %pad_clamp_fusion.1), kind=kCustom, calls=%fused_computation | custom fusion | bytes 786944 | tf_op jit(solution)/shard_map/jit(_take)/gather | solution.py:30
  374.1 0.1 select_select_fusion
  374.3 0.1 select_select_fusion.1
  374.5 3.7 collective-permute-start
  378.1 21.8 %collective-permute-done = f32[320,768]{1,0:T(8,128)S(1)} collective-permute-done((f32[320,768]{1,0:T(8,128)S(1)}, f32[320,768]{1,0:T(8,128)S(1)}, u32[]{:S(2)}, u32[]{:S(2)}) %collective-permute-start) | collective-permute-done | bytes 983072 | tf_op jit(solution)/shard_map/ppermute | solution.py:35
  400.0 0.1 fusion.4
  400.1 1.6 collective-permute-start.1
  401.7 1.7 collective-permute-start.2
  403.4 21.1 %collective-permute-done.1 = f32[320,768]{1,0:T(8,128)S(1)} collective-permute-done((f32[320,768]{1,0:T(8,128)S(1)}, f32[320,768]{1,0:T(8,128)S(1)}, u32[]{:S(2)}, u32[]{:S(2)}) %collective-permute-start.1) | collective-permute-done | bytes 983072 | tf_op jit(solution)/shard_map/ppermute | solution.py:35
  424.4 0.3 collective-permute-start.3
  424.7 23.1 %collective-permute-done.3 = f32[320,768]{1,0:T(8,128)S(1)} collective-permute-done((f32[320,768]{1,0:T(8,128)S(1)}, f32[320,768]{1,0:T(8,128)S(1)}, u32[]{:S(2)}, u32[]{:S(2)}) %collective-permute-start.3) | collective-permute-done | bytes 983072 | tf_op jit(solution)/shard_map/ppermute | solution.py:35
  447.8 0.2 add_add_fusion
  448.1 16.5 %convolution_reduce_fusion = f32[8192]{0:T(1024)S(1)} fusion(f32[8192,768]{1,0:T(8,128)} %bitcast, f32[320,768]{1,0:T(8,128)S(1)} %add_add_fusion), kind=kOutput, calls=%fused_computation.5 | convolution fusion | flops 4832878592 | bytes 25591808 | tf_op jit(solution)/shard_map/dot_general | solution.py:18
  464.6 1.2 collective-permute-done.4
  465.8 2.5 collective-permute-start.5
  468.3 0.8 collective-permute-start.6
  469.1 1.9 collective-permute-done.5
  471.0 1.3 collective-permute-done.6
  472.2 0.1 collective-permute-start.7
  472.4 5.0 collective-permute-done.7
  477.4 3.9 collective-permute-done.8
  481.4 17.4 %fusion.1 = f32[192]{0:T(256)S(1)} fusion(f32[8192]{0:T(1024)S(1)} %maximum_maximum_fusion, f32[8192,768]{1,0:T(8,128)} %bitcast, f32[320,768]{1,0:T(8,128)S(1)} %add_add_fusion), kind=kOutput, calls=%fused_computation.4 | convolution fusion | flops 7252475904 | bytes 25789184 | tf_op jit(solution)/shard_map/dot_general | solution.py:18
  498.8 2.7 collective-permute-start.9
  501.4 2.5 collective-permute-done.9
  504.0 3.2 collective-permute-start.10
  507.2 1.6 collective-permute-done.11
  508.8 4.8 collective-permute-done.12
  513.6 0.6 dynamic-slice_reduce_fusion
  (29 shorter events, 0.4 us)
Async XLA Ops:
  12.8 6.0 %copy-start.2 = (s32[192]{0:T(256)S(1)}, s32[192]{0:T(256)}, u32[]{:S(2)}) copy-start(s32[192]{0:T(256)} %param.7) | copy-start | bytes 2308
  12.8 6.1 %copy-start.3 = (s32[128]{0:T(128)S(1)}, s32[128]{0:T(128)}, u32[]{:S(2)}) copy-start(s32[128]{0:T(128)} %param.6) | copy-start | bytes 1540
  12.8 342.9 %all-to-all-start = ((f32[16,512,768]{2,1,0:T(8,128)}), f32[16,512,768]{2,1,0:T(8,128)}, u32[]{:S(2)}, u32[]{:S(2)}) async-start(f32[16,512,768]{2,1,0:T(8,128)} %stack.24), calls=%async_computation | async-start | bytes 50331648 | tf_op jit(solution)/shard_map/all_to_all | solution.py:9
  365.0 116.4 %copy-start.1 = (f32[8192]{0:T(1024)S(1)}, f32[8192]{0:T(1024)}, u32[]{:S(2)}) copy-start(f32[8192]{0:T(1024)} %param.5) | copy-start | bytes 98308
  374.5 25.5 %collective-permute-start = (f32[320,768]{1,0:T(8,128)S(1)}, f32[320,768]{1,0:T(8,128)S(1)}, u32[]{:S(2)}, u32[]{:S(2)}) collective-permute-start(f32[320,768]{1,0:T(8,128)S(1)} %pad_maximum_fusion), channel_id=1, source_target_pairs={{0,1},{1,0},{2,3},{3,2},{4,5},{5,4},{6,7},{7,6},{8,9},{9,8},{10,11... | collective-permute-start | bytes 2949128 | tf_op jit(solution)/shard_map/ppermute | solution.py:35
  400.1 24.4 %collective-permute-start.1 = (f32[320,768]{1,0:T(8,128)S(1)}, f32[320,768]{1,0:T(8,128)S(1)}, u32[]{:S(2)}, u32[]{:S(2)}) collective-permute-start(f32[320,768]{1,0:T(8,128)S(1)} %fusion.4), channel_id=1, source_target_pairs={{0,2},{1,3},{2,4},{3,5},{4,6},{5,7},{6,0},{7,1},{8,10},{9,11},{10,... | collective-permute-start | bytes 2949128 | tf_op jit(solution)/shard_map/ppermute | solution.py:35
  401.7 23.0 %collective-permute-start.2 = (f32[320,768]{1,0:T(8,128)S(1)}, f32[320,768]{1,0:T(8,128)S(1)}, u32[]{:S(2)}, u32[]{:S(2)}) collective-permute-start(f32[320,768]{1,0:T(8,128)S(1)} %fusion.4), channel_id=1, source_target_pairs={{0,6},{1,7},{2,0},{3,1},{4,2},{5,3},{6,4},{7,5},{8,14},{9,15},{10,... | collective-permute-start | bytes 2949128 | tf_op jit(solution)/shard_map/ppermute | solution.py:35
  424.4 23.4 %collective-permute-start.3 = (f32[320,768]{1,0:T(8,128)S(1)}, f32[320,768]{1,0:T(8,128)S(1)}, u32[]{:S(2)}, u32[]{:S(2)}) collective-permute-start(f32[320,768]{1,0:T(8,128)S(1)} %collective-permute-done.1), channel_id=1, source_target_pairs={{0,2},{1,3},{2,4},{3,5},{4,6},{5,7},{6,0},{7,1},{8,10},{9,11},{10,... | collective-permute-start | bytes 2949128 | tf_op jit(solution)/shard_map/ppermute | solution.py:35
  464.5 1.3 collective-permute-start.4
  465.8 5.1 collective-permute-start.5
  468.3 3.9 collective-permute-start.6
  472.2 5.2 %collective-permute-start.7 = (f32[8192]{0:T(1024)S(1)}, f32[8192]{0:T(1024)S(1)}, u32[]{:S(2)}, u32[]{:S(2)}) collective-permute-start(f32[8192]{0:T(1024)S(1)} %maximum_maximum_fusion.1), channel_id=1, source_target_pairs={{0,16},{8,24},{16,32},{24,40},{32,48},{40,56},{48,0},{56,8},{64,80... | collective-permute-start | bytes 98312 | tf_op jit(solution)/shard_map/ppermute | solution.py:35
  477.4 3.9 collective-permute-start.8
  481.4 32.9 %copy-start = (f32[8192]{0:T(1024)}, f32[8192]{0:T(1024)S(1)}, u32[]{:S(2)}) copy-start(f32[8192]{0:T(1024)S(1)} %maximum_maximum_fusion) | copy-start | bytes 98308
  498.8 5.2 %collective-permute-start.9 = (f32[192]{0:T(256)S(1)}, f32[192]{0:T(256)S(1)}, u32[]{:S(2)}, u32[]{:S(2)}) collective-permute-start(f32[192]{0:T(256)S(1)} %fusion.1), channel_id=1, source_target_pairs={{0,1},{1,0},{2,3},{3,2},{4,5},{5,4},{6,7},{7,6},{8,9},{9,8},{10,11... | collective-permute-start | bytes 2312 | tf_op jit(solution)/shard_map/ppermute | solution.py:35
  503.9 4.9 collective-permute-start.11
  504.0 4.8 collective-permute-start.10
  508.8 4.8 collective-permute-start.12
